TPU v7x, 32 devices: a whole 2x2x4 slice. The times are simulated.
32 devices in a mesh: rep: 2 (over x), member: 4 (over y, core), tp: 4 (over z).
Axes of the slice: x: 2, y: 2, z: 4, core: 2. Of those that a mesh axis runs over, the one named last changes fastest.
Arguments:
- states: bfloat16 [4096, 1024], P(('rep', 'member', 'tp')), parts along dimension 0, may hold values from -6 to 6
- member_of: int32 [4096, 1], P(('rep', 'member', 'tp')), parts along dimension 0, may hold values from 0 to 1; in each aligned block of 128 rows (0 to 127, 128 to 255, ...) at most 128 rows name the same one
- place: int32 [4096], P(('rep', 'member', 'tp')), parts along dimension 0, may hold values from 0 to 2047, as said below
- norm_gain: float32 [2, 1024], replicated, may hold values from 0.5 to 2
- w_up: bfloat16 [4, 1024, 2048], P('member', None, 'tp'), may hold values from -0.1875 to 0.1875
- w_down: bfloat16 [4, 2048, 1024], P('member', 'tp'), may hold values from -0.09375 to 0.09375
- policy_gain: float32 [1024], replicated, may hold values from 0.5 to 2
- w_policy: bfloat16 [1024, 128], replicated, may hold values from -0.1875 to 0.1875
Outputs:
- imagined: bfloat16 [4096, 1024], P(('rep', 'member', 'tp')), parts along dimension 0
- action: bfloat16 [4096, 128], P(('rep', 'member', 'tp')), parts along dimension 0
There are 2 independent parts, one for each index of `rep`. A program takes and returns all parts, laid end to end along the dimension named above; an argument that names none is the same for every part. Nothing has to cross between parts.
Inputs may be any that keep to these rules, and one draw needn't show every extreme that they name: `member_of`: at most 128 of the rows of one device name any one member, and that count is reached on some device. `place`: A permutation of the 2048 learner positions; learner device k holds positions k * 128 to (k + 1) * 128 - 1, and the rows of each device go exactly 8 to every learner device.
All inputs are finite; a program needn't handle non-finite values.
Results may differ from a plain program's by a relative error of at most 0.0069.
Values may be sent and summed in bfloat16 or wider, within the bound.
No kernel may reach another device: no remote copies, remote signals or barrier semaphores. Data moves between devices by JAX's collectives and lax.ppermute only.
A program may use at most 128 MiB of HBM per device.

v0:
```python
import jax
import jax.numpy as jnp
from jax import lax
from jax.sharding import PartitionSpec as P


def from_partner(value, axis, distance):
    return lax.ppermute(value, axis, [(i, i ^ 1 << distance) for i in range(lax.axis_size(axis))])


def rms_scale(values, gain):
    mean_square = jnp.mean(values * values, axis=-1, keepdims=True)
    return values * lax.rsqrt(mean_square + 1e-06) * gain


def running_rank(member_hits):
    return jnp.sum((jnp.cumsum(member_hits, axis=0) - member_hits) * member_hits, axis=1)


def local(states, member_of, place, norm_gain, w_up, w_down, policy_gain, w_policy):
    n_member = lax.axis_size("member")
    n_tp = lax.axis_size("tp")
    n_dev = n_member * n_tp
    group_width = 2 * n_tp
    member_total = n_member // 2
    rows_here = states.shape[0]
    feature_width = states.shape[1]
    slot_count = 2 * rows_here // n_dev
    member = member_of[:, 0]
    member_hits = (member[:, None] == jnp.arange(member_total, dtype=jnp.int32)[None, :]).astype(
        jnp.int32
    )
    earlier = running_rank(member_hits)
    target = (member * group_width + earlier % group_width) * slot_count + earlier // group_width
    picker = (jnp.arange(n_dev * slot_count, dtype=jnp.int32)[:, None] == target[None, :]).astype(
        jnp.bfloat16
    )
    outgoing = jnp.dot(picker, states, preferred_element_type=jnp.float32).astype(jnp.bfloat16)
    arrived = lax.all_to_all(
        outgoing.reshape(n_dev, slot_count, feature_width),
        ("member", "tp"),
        split_axis=0,
        concat_axis=0,
        tiled=True,
    )
    arrived = arrived.reshape(n_dev * slot_count, feature_width)
    own_member = lax.axis_index("member") // 2
    gain_here = lax.dynamic_index_in_dim(norm_gain, own_member, 0, keepdims=False)
    normed = rms_scale(arrived.astype(jnp.float32), gain_here).astype(jnp.bfloat16)
    up_local = jnp.concatenate([w_up[0], from_partner(w_up[0], "member", 0)], axis=1)
    down_local = jnp.concatenate([w_down[0], from_partner(w_down[0], "member", 0)], axis=0)
    hidden = jax.nn.gelu(
        jnp.dot(
            lax.all_gather(normed, "tp", axis=0, tiled=True),
            up_local,
            preferred_element_type=jnp.float32,
        )
    ).astype(jnp.bfloat16)
    change = lax.psum_scatter(
        jnp.dot(hidden, down_local, preferred_element_type=jnp.float32),
        "tp",
        scatter_dimension=0,
        tiled=True,
    )
    predicted = (arrived.astype(jnp.float32) + change).astype(jnp.bfloat16)
    returned = lax.all_to_all(
        predicted.reshape(n_dev, slot_count, feature_width),
        ("member", "tp"),
        split_axis=0,
        concat_axis=0,
        tiled=True,
    )
    returned = returned.reshape(n_dev * slot_count, feature_width)
    own_rows = jnp.einsum("sr,sd->rd", picker, returned, preferred_element_type=jnp.float32).astype(
        jnp.bfloat16
    )
    per_learner = rows_here // n_dev
    learner = place // rows_here
    spot_index = place % rows_here
    learner_hits = (learner[:, None] == jnp.arange(n_dev, dtype=jnp.int32)[None, :]).astype(
        jnp.int32
    )
    lane_index = learner * per_learner + running_rank(learner_hits)
    placer = jnp.arange(rows_here, dtype=jnp.int32)[:, None] == lane_index[None, :]
    packed = jnp.dot(
        placer.astype(jnp.bfloat16), own_rows, preferred_element_type=jnp.float32
    ).astype(jnp.bfloat16)
    packed_spot = jnp.sum(placer.astype(jnp.int32) * spot_index[None, :], axis=1)
    arrivals, arrival_spots = (
        lax.all_to_all(
            packed.reshape(n_dev, per_learner, feature_width),
            ("member", "tp"),
            split_axis=0,
            concat_axis=0,
            tiled=True,
        ),
        lax.all_to_all(
            packed_spot.reshape(n_dev, per_learner),
            ("member", "tp"),
            split_axis=0,
            concat_axis=0,
            tiled=True,
        ),
    )
    arrivals = arrivals.reshape(rows_here, feature_width)
    arrival_spots = arrival_spots.reshape(rows_here)
    settle = (jnp.arange(rows_here, dtype=jnp.int32)[:, None] == arrival_spots[None, :]).astype(
        jnp.bfloat16
    )
    imagined = jnp.dot(settle, arrivals, preferred_element_type=jnp.float32).astype(jnp.bfloat16)
    policy_normed = rms_scale(imagined.astype(jnp.float32), policy_gain).astype(jnp.bfloat16)
    action = jnp.tanh(jnp.dot(policy_normed, w_policy, preferred_element_type=jnp.float32)).astype(
        jnp.bfloat16
    )
    return (imagined, action)


def solution(mesh):
    in_specs = (
        P(("rep", "member", "tp"), None),
        P(("rep", "member", "tp"), None),
        P(("rep", "member", "tp")),
        P(),
        P("member", None, "tp"),
        P("member", "tp", None),
        P(),
        P(),
    )
    out_specs = (P(("rep", "member", "tp"), None), P(("rep", "member", "tp"), None))
    return jax.shard_map(local, mesh=mesh, in_specs=in_specs, out_specs=out_specs, check_vma=False)
```

profile of v0, /device:TPU:0, one launch (start us, length us, event | category | flops | bytes accessed | tf_op | source)
XLA Modules:
  0.0 218.8 jit_solution(4283796861576501177)
XLA Ops:
  7.2 0.9 fusion.41
  8.3 0.8 select_reduce_fusion
  9.1 0.7 multiply_add_fusion
  9.8 1.1 convolution_convert_fusion
  10.9 7.4 %all-to-all-start.1 = ((bf16[16,16,1024]{2,1,0:T(8,128)(2,1)}), bf16[16,16,1024]{2,1,0:T(8,128)(2,1)S(1)}, u32[]{:S(2)}, u32[]{:S(2)}) async-start(bf16[16,16,1024]{2,1,0:T(8,128)(2,1)} %bitcast.2), calls=%async_computation.1 | async-start | bytes 1048576 | tf_op jit(solution)/shard_map/all_to_all | solution.py:39
  18.3 0.7 constant_dynamic-slice_fusion
  19.0 14.9 %all-to-all-done.1 = bf16[16,16,1024]{2,1,0:T(8,128)(2,1)S(1)} async-done(((bf16[16,16,1024]{2,1,0:T(8,128)(2,1)}), bf16[16,16,1024]{2,1,0:T(8,128)(2,1)S(1)}, u32[]{:S(2)}, u32[]{:S(2)}) %all-to-all-start.1) | async-done | bytes 524320 | tf_op jit(solution)/shard_map/all_to_all | solution.py:39
  34.2 1.0 fusion.29
  35.9 2.8 %collective-permute-done = bf16[1024,512]{1,0:T(8,128)(2,1)S(1)} collective-permute-done((bf16[1024,512]{1,0:T(8,128)(2,1)S(1)}, bf16[1024,512]{1,0:T(8,128)(2,1)S(1)}, u32[]{:S(2)}, u32[]{:S(2)}) %collective-permute-start) | collective-permute-done | bytes 1048608 | tf_op jit(solution)/shard_map/ppermute | solution.py:8
  38.6 1.0 copy-done.4
  39.6 40.4 %all-gather.2.cloned.1.call-done = bf16[1024,1024]{1,0:T(8,128)(2,1)} async-done(((bf16[256,1024]{1,0:T(8,128)(2,1)}), bf16[1024,1024]{1,0:T(8,128)(2,1)}) %all-gather.2.cloned.1.call-update) | async-done | bytes 2097168 | tf_op jit(solution)/shard_map/all_gather | solution.py:54
  80.0 8.7 %fusion.8 = f32[1024,1024]{1,0:T(8,128)} fusion(bf16[512,1024]{1,0:T(8,128)(2,1)} %collective-permute-done.1, bf16[512,1024]{1,0:T(8,128)(2,1)S(1)} %bitcast.34, bf16[1024,1024]{1,0:T(8,128)(2,1)} %all-gather.2.cloned.1.call-done, bf16[1024,512]{1,0:T(8,128)(2,1)} %copy-done.4, bf16[1024,512]{1,0:T(8,128)(2,1)S(1)} %bitcast.36), kind=kOutput, calls=%fused_computation.9 | convolution fusion | flops 4312793088 | bytes 10485760 | tf_op jit(solution)/shard_map/dot_general | solution.py:60
  88.7 75.6 %reduce-scatter.2.cloned.1.call-done = f32[256,1024]{1,0:T(8,128)} async-done(((f32[1024,1024]{1,0:T(8,128)}), f32[256,1024]{1,0:T(8,128)}) %reduce-scatter.2.cloned.1.call-update) | async-done | bytes 1048592 | tf_op jit(solution)/shard_map/reduce_scatter | solution.py:59
  164.4 2.2 fusion.30
  166.5 5.2 %all-to-all-start.2 = ((bf16[16,16,1024]{2,1,0:T(8,128)(2,1)}), bf16[16,16,1024]{2,1,0:T(8,128)(2,1)S(1)}, u32[]{:S(2)}, u32[]{:S(2)}) async-start(bf16[16,16,1024]{2,1,0:T(8,128)(2,1)} %bitcast.7), calls=%async_computation.3 | async-start | bytes 1048576 | tf_op jit(solution)/shard_map/all_to_all | solution.py:66
  172.4 0.7 all_to_all.15
  173.1 14.4 %all-to-all-done.2 = bf16[16,16,1024]{2,1,0:T(8,128)(2,1)S(1)} async-done(((bf16[16,16,1024]{2,1,0:T(8,128)(2,1)}), bf16[16,16,1024]{2,1,0:T(8,128)(2,1)S(1)}, u32[]{:S(2)}, u32[]{:S(2)}) %all-to-all-start.2) | async-done | bytes 524320 | tf_op jit(solution)/shard_map/all_to_all | solution.py:66
  187.5 3.5 %all-to-all-start = ((s32[16,1,8]{2,1,0:T(1,128)}), s32[16,1,8]{2,1,0:T(1,128)S(1)}, u32[]{:S(2)}, u32[]{:S(2)}) async-start(s32[16,1,8]{2,1,0:T(1,128)} %bitcast), calls=%async_computation | async-start | bytes 16384 | tf_op jit(solution)/shard_map/all_to_all | solution.py:97
  190.9 1.2 fusion.25
  192.1 5.1 %all-to-all-done = s32[16,1,8]{2,1,0:T(1,128)S(1)} async-done(((s32[16,1,8]{2,1,0:T(1,128)}), s32[16,1,8]{2,1,0:T(1,128)S(1)}, u32[]{:S(2)}, u32[]{:S(2)}) %all-to-all-start) | async-done | bytes 544 | tf_op jit(solution)/shard_map/all_to_all | solution.py:97
  197.2 3.5 %all-to-all-start.3 = ((bf16[16,8,1024]{2,1,0:T(8,128)(2,1)}), bf16[16,8,1024]{2,1,0:T(8,128)(2,1)S(1)}, u32[]{:S(2)}, u32[]{:S(2)}) async-start(bf16[16,8,1024]{2,1,0:T(8,128)(2,1)} %fusion.25), calls=%async_computation.4 | async-start | bytes 524288 | tf_op jit(solution)/shard_map/all_to_all | solution.py:90
  201.2 0.7 reduce.4
  202.0 8.7 %all-to-all-done.3 = bf16[16,8,1024]{2,1,0:T(8,128)(2,1)S(1)} async-done(((bf16[16,8,1024]{2,1,0:T(8,128)(2,1)}), bf16[16,8,1024]{2,1,0:T(8,128)(2,1)S(1)}, u32[]{:S(2)}, u32[]{:S(2)}) %all-to-all-start.3) | async-done | bytes 262176 | tf_op jit(solution)/shard_map/all_to_all | solution.py:90
  211.1 0.9 fusion.26
  (36 shorter events, 2.7 us)
Async XLA Ops:
  7.2 2.6 %copy-start = (bf16[128,1024]{1,0:T(8,128)(2,1)S(1)}, bf16[128,1024]{1,0:T(8,128)(2,1)}, u32[]{:S(2)}) copy-start(bf16[128,1024]{1,0:T(8,128)(2,1)} %param.8) | copy-start | bytes 786436
  7.2 28.1 %copy-start.3 = (bf16[1,1024,512]{2,1,0:T(8,128)(2,1)S(1)}, bf16[1,1024,512]{2,1,0:T(8,128)(2,1)}, u32[]{:S(2)}) copy-start(bf16[1,1024,512]{2,1,0:T(8,128)(2,1)} %param.12) | copy-start | bytes 3145732
  7.2 28.2 %copy-start.2 = (bf16[1,512,1024]{2,1,0:T(8,128)(2,1)S(1)}, bf16[1,512,1024]{2,1,0:T(8,128)(2,1)}, u32[]{:S(2)}) copy-start(bf16[1,512,1024]{2,1,0:T(8,128)(2,1)} %param.13) | copy-start | bytes 3145732
  10.9 23.1 %all-to-all-start.1 = ((bf16[16,16,1024]{2,1,0:T(8,128)(2,1)}), bf16[16,16,1024]{2,1,0:T(8,128)(2,1)S(1)}, u32[]{:S(2)}, u32[]{:S(2)}) async-start(bf16[16,16,1024]{2,1,0:T(8,128)(2,1)} %bitcast.2), calls=%async_computation.1 | async-start | bytes 1048576 | tf_op jit(solution)/shard_map/all_to_all | solution.py:39
  18.3 61.7 %all-gather.2.cloned.1.call-start = ((), (), s32[]{:S(2)}) async-start(), calls=%async_computation.5 | async-start | bytes 2621440 | tf_op jit(solution)/shard_map/all_gather | solution.py:54
  35.2 129.1 %reduce-scatter.2.cloned.1.call-start = ((), (), s32[]{:S(2)}) async-start(), calls=%async_computation.6 | async-start | bytes 5242880 | tf_op jit(solution)/shard_map/reduce_scatter | solution.py:59
  35.3 3.3 %collective-permute-start = (bf16[1024,512]{1,0:T(8,128)(2,1)S(1)}, bf16[1024,512]{1,0:T(8,128)(2,1)S(1)}, u32[]{:S(2)}, u32[]{:S(2)}) collective-permute-start(bf16[1024,512]{1,0:T(8,128)(2,1)S(1)} %bitcast.35), channel_id=1, source_target_pairs={{0,4},{4,0},{8,12},{12,8},{1,5},{5,1},{9,13},{13,9},{2,6},{6,2},{1... | collective-permute-start | bytes 3145736 | tf_op jit(solution)/shard_map/ppermute | solution.py:8
  35.4 4.3 %collective-permute-start.1 = (bf16[512,1024]{1,0:T(8,128)(2,1)S(1)}, bf16[512,1024]{1,0:T(8,128)(2,1)}, u32[]{:S(2)}, u32[]{:S(2)}) collective-permute-start(bf16[512,1024]{1,0:T(8,128)(2,1)S(1)} %bitcast.33), channel_id=1, source_target_pairs={{0,4},{4,0},{8,12},{12,8},{1,5},{5,1},{9,13},{13,9},{2,6},{6,2},{1... | collective-permute-start | bytes 3145736 | tf_op jit(solution)/shard_map/ppermute | solution.py:8
  38.6 1.0 copy-start.4
  88.7 83.1 %copy-start.7 = (s32[128]{0:T(128)S(1)}, s32[128]{0:T(128)}, u32[]{:S(2)}) copy-start(s32[128]{0:T(128)} %param.10) | copy-start | bytes 1540
  88.7 122.4 %copy-start.5 = (bf16[1024,128]{1,0:T(8,128)(2,1)S(1)}, bf16[1024,128]{1,0:T(8,128)(2,1)}, u32[]{:S(2)}) copy-start(bf16[1024,128]{1,0:T(8,128)(2,1)} %param.15) | copy-start | bytes 786436
  88.7 122.4 %copy-start.6 = (f32[1024]{0:T(1024)S(1)}, f32[1024]{0:T(1024)}, u32[]{:S(2)}) copy-start(f32[1024]{0:T(1024)} %param.14) | copy-start | bytes 12292
  166.5 20.9 %all-to-all-start.2 = ((bf16[16,16,1024]{2,1,0:T(8,128)(2,1)}), bf16[16,16,1024]{2,1,0:T(8,128)(2,1)S(1)}, u32[]{:S(2)}, u32[]{:S(2)}) async-start(bf16[16,16,1024]{2,1,0:T(8,128)(2,1)} %bitcast.7), calls=%async_computation.3 | async-start | bytes 1048576 | tf_op jit(solution)/shard_map/all_to_all | solution.py:66
  187.5 9.7 %all-to-all-start = ((s32[16,1,8]{2,1,0:T(1,128)}), s32[16,1,8]{2,1,0:T(1,128)S(1)}, u32[]{:S(2)}, u32[]{:S(2)}) async-start(s32[16,1,8]{2,1,0:T(1,128)} %bitcast), calls=%async_computation | async-start | bytes 16384 | tf_op jit(solution)/shard_map/all_to_all | solution.py:97
  197.2 13.6 %all-to-all-start.3 = ((bf16[16,8,1024]{2,1,0:T(8,128)(2,1)}), bf16[16,8,1024]{2,1,0:T(8,128)(2,1)S(1)}, u32[]{:S(2)}, u32[]{:S(2)}) async-start(bf16[16,8,1024]{2,1,0:T(8,128)(2,1)} %fusion.25), calls=%async_computation.4 | async-start | bytes 524288 | tf_op jit(solution)/shard_map/all_to_all | solution.py:90
  211.0 1.0 copy-start.1
Sparse Core Ops, SparseCore 0:
  35.4 44.6 all-gather.1
  88.9 75.4 reduce-scatter.1
where the time goes:
time: 219 us
  waiting for transfers between devices  162 us (74%)
  starting transfers between devices  20.2 us (9%)
  between operations  14.2 us (6%)
  matrix products  12.2 us (6%)
  other arithmetic  7.14 us (3%)
  local copies, waits for them, and re-layouts  3.1 us (1%)
    reduce_scatter x1, waiting for transfers between devices, local(): lax.psum_scatter(jnp.dot(hidden, down_local, preferred_element_type=jnp.f...  75.6 us
    all_gather x1, waiting for transfers between devices, local(): lax.all_gather(normed, 'tp', axis=0, tiled=True)  40.4 us
    all_to_all x1, waiting for transfers between devices, local(): lax.all_to_all(outgoing.reshape(n_dev, slot_count, feature_width), ('memb...  14.9 us
    all_to_all x1, waiting for transfers between devices, local(): lax.all_to_all(predicted.reshape(n_dev, slot_count, feature_width), ('mem...  14.4 us
    all_to_all x1, waiting for transfers between devices, local(): lax.all_to_all(packed.reshape(n_dev, per_learner, feature_width), ('membe...  8.74 us
    dot_general x1, matrix products, local(): jnp.dot(hidden, down_local, preferred_element_type=jnp.float32)  8.7 us
    all_to_all x1, starting transfers between devices, local(): lax.all_to_all(outgoing.reshape(n_dev, slot_count, feature_width), ('memb...  7.39 us
    all_to_all x1, starting transfers between devices, local(): lax.all_to_all(predicted.reshape(n_dev, slot_count, feature_width), ('mem...  5.21 us
  transfers between devices with their start and end apart: 8, of which 7 were waited for; matrix products, arithmetic and copies ran while one was open for 2% of the time, Pallas kernels for 0%

commit v1 on v0

--- a/solution.py
+++ b/solution.py
@@ -2,6 +2,22 @@
 import jax.numpy as jnp
 from jax import lax
 from jax.sharding import PartitionSpec as P
+
+
+def collect(x, axis, dim):
+    ways, here, step = (lax.axis_size(axis), lax.axis_index(axis), x.shape[dim])
+    shape = [n * ways if d == dim else n for d, n in enumerate(x.shape)]
+    full = lax.dynamic_update_slice_in_dim(jnp.zeros(shape, x.dtype), x, here * step, axis=dim)
+    going_up = going_down = x
+    for far in range(1, ways // 2 + 1):
+        going_up = lax.ppermute(going_up, axis, [(d, (d + 1) % ways) for d in range(ways)])
+        full = lax.dynamic_update_slice_in_dim(full, going_up, (here - far) % ways * step, axis=dim)
+        if 2 * far < ways:
+            going_down = lax.ppermute(going_down, axis, [(d, (d - 1) % ways) for d in range(ways)])
+            full = lax.dynamic_update_slice_in_dim(
+                full, going_down, (here + far) % ways * step, axis=dim
+            )
+    return full
 
 
 def from_partner(value, axis, distance):
@@ -50,11 +66,7 @@
     up_local = jnp.concatenate([w_up[0], from_partner(w_up[0], "member", 0)], axis=1)
     down_local = jnp.concatenate([w_down[0], from_partner(w_down[0], "member", 0)], axis=0)
     hidden = jax.nn.gelu(
-        jnp.dot(
-            lax.all_gather(normed, "tp", axis=0, tiled=True),
-            up_local,
-            preferred_element_type=jnp.float32,
-        )
+        jnp.dot(collect(normed, "tp", 0), up_local, preferred_element_type=jnp.float32)
     ).astype(jnp.bfloat16)
     change = lax.psum_scatter(
         jnp.dot(hidden, down_local, preferred_element_type=jnp.float32),

time: 219 us -> 212 us (0.968)
  waiting for transfers between devices: 162 us -> 150 us
  starting transfers between devices: 20.2 us -> 24.2 us
    all_gather x1 -> x0, waiting for transfers between devices: 40.4 us -> none  [local(): lax.all_gather(normed, 'tp', axis=0, tiled=True)]
    ppermute x0 -> x3, waiting for transfers between devices: none -> 31.4 us  [the longest x2 23 us: collect(): lax.ppermute(going_up, axis, [(d, (d + 1) % ways) for d in range(ways)])]
    ppermute x0 -> x3, starting transfers between devices: none -> 3.81 us  [the longest x1 3.74 us: collect(): lax.ppermute(going_down, axis, [(d, (d - 1) % ways) for d in range(ways)])]
    dynamic_update_slice x0 -> x3, local copies, waits for them, and re-layouts: none -> 3.26 us  [the longest x2 2.19 us: collect(): lax.dynamic_update_slice_in_dim(full, going_up, (here - far) % ways * ste...]
    ppermute x2, waiting for transfers between devices: 2.8 us -> 0.01 us  [from_partner(): lax.ppermute(value, axis, [(i, i ^ 1 << distance) for i in range(lax.axis...]
  transfers between devices with their start and end apart: 8 -> 10, of which waited for: 7 -> 8; matrix products, arithmetic and copies ran while one was open for 2% -> 3% of each run, Pallas kernels for 0% -> 0%
where the time goes in v1:
time: 212 us
  waiting for transfers between devices  150 us (71%)
  starting transfers between devices  24.2 us (11%)
  between operations  14.3 us (7%)
  matrix products  12.1 us (6%)
  other arithmetic  6.24 us (3%)
  local copies, waits for them, and re-layouts  4.94 us (2%)
    reduce_scatter x1, waiting for transfers between devices, local(): lax.psum_scatter(jnp.dot(hidden, down_local, preferred_element_type=jnp.f...  74.8 us
    ppermute x2, waiting for transfers between devices, collect(): lax.ppermute(going_up, axis, [(d, (d + 1) % ways) for d in range(ways)])  23 us
    all_to_all x1, waiting for transfers between devices, local(): lax.all_to_all(outgoing.reshape(n_dev, slot_count, feature_width), ('memb...  15.6 us
    all_to_all x1, waiting for transfers between devices, local(): lax.all_to_all(predicted.reshape(n_dev, slot_count, feature_width), ('mem...  14.4 us
    all_to_all x1, waiting for transfers between devices, local(): lax.all_to_all(packed.reshape(n_dev, per_learner, feature_width), ('membe...  8.74 us
    dot_general x1, matrix products, local(): jnp.dot(hidden, down_local, preferred_element_type=jnp.float32)  8.68 us
    ppermute x1, waiting for transfers between devices, collect(): lax.ppermute(going_down, axis, [(d, (d - 1) % ways) for d in range(ways)])  8.4 us
    all_to_all x1, starting transfers between devices, local(): lax.all_to_all(outgoing.reshape(n_dev, slot_count, feature_width), ('memb...  7.39 us
  transfers between devices with their start and end apart: 10, of which 8 were waited for; matrix products, arithmetic and copies ran while one was open for 3% of the time, Pallas kernels for 0%

profile of v1, /device:TPU:0, one launch (start us, length us, event | category | flops | bytes accessed | tf_op | source)
XLA Modules:
  0.0 211.8 jit_solution(2933221774789861390)
XLA Ops:
  7.2 0.8 fusion.41
  8.1 0.8 select_reduce_fusion
  9.7 1.1 convolution_convert_fusion
  10.8 7.4 %all-to-all-start.1 = ((bf16[16,16,1024]{2,1,0:T(8,128)(2,1)}), bf16[16,16,1024]{2,1,0:T(8,128)(2,1)S(1)}, u32[]{:S(2)}, u32[]{:S(2)}) async-start(bf16[16,16,1024]{2,1,0:T(8,128)(2,1)} %bitcast.2), calls=%async_computation.1 | async-start | bytes 1048576 | tf_op jit(solution)/shard_map/all_to_all | solution.py:55
  18.3 15.6 %all-to-all-done.1 = bf16[16,16,1024]{2,1,0:T(8,128)(2,1)S(1)} async-done(((bf16[16,16,1024]{2,1,0:T(8,128)(2,1)}), bf16[16,16,1024]{2,1,0:T(8,128)(2,1)S(1)}, u32[]{:S(2)}, u32[]{:S(2)}) %all-to-all-start.1) | async-done | bytes 524320 | tf_op jit(solution)/shard_map/all_to_all | solution.py:55
  35.2 3.7 %collective-permute-start.1 = (bf16[256,1024]{1,0:T(8,128)(2,1)S(1)}, bf16[256,1024]{1,0:T(8,128)(2,1)}, u32[]{:S(2)}, u32[]{:S(2)}) collective-permute-start(bf16[256,1024]{1,0:T(8,128)(2,1)S(1)} %get-tuple-element.5), channel_id=1, source_target_pairs={{0,3},{1,0},{2,1},{3,2},{4,7},{5,4},{6,5},{7,6},{8,11},{9,8},{10,9... | collective-permute-start | bytes 1572872 | tf_op jit(solution)/shard_map/ppermute | solution.py:16
  39.0 12.4 %collective-permute-done = bf16[256,1024]{1,0:T(8,128)(2,1)} collective-permute-done((bf16[256,1024]{1,0:T(8,128)(2,1)S(1)}, bf16[256,1024]{1,0:T(8,128)(2,1)}, u32[]{:S(2)}, u32[]{:S(2)}) %collective-permute-start) | collective-permute-done | bytes 524320 | tf_op jit(solution)/shard_map/ppermute | solution.py:13
  51.4 1.1 constant_dynamic-update-slice_fusion.1
  52.5 8.4 %collective-permute-done.1 = bf16[256,1024]{1,0:T(8,128)(2,1)} collective-permute-done((bf16[256,1024]{1,0:T(8,128)(2,1)S(1)}, bf16[256,1024]{1,0:T(8,128)(2,1)}, u32[]{:S(2)}, u32[]{:S(2)}) %collective-permute-start.1) | collective-permute-done | bytes 524320 | tf_op jit(solution)/shard_map/ppermute | solution.py:16
  60.9 1.1 constant_dynamic-update-slice_fusion
  62.0 10.6 %collective-permute-done.2 = bf16[256,1024]{1,0:T(8,128)(2,1)} collective-permute-done((bf16[256,1024]{1,0:T(8,128)(2,1)}, bf16[256,1024]{1,0:T(8,128)(2,1)}, u32[]{:S(2)}, u32[]{:S(2)}) %collective-permute-start.2) | collective-permute-done | bytes 524320 | tf_op jit(solution)/shard_map/ppermute | solution.py:13
  72.6 1.1 constant_dynamic-update-slice_fusion.3
  73.7 8.7 %fusion.8 = f32[1024,1024]{1,0:T(8,128)} fusion(bf16[512,1024]{1,0:T(8,128)(2,1)} %collective-permute-done.4, bf16[512,1024]{1,0:T(8,128)(2,1)} %bitcast.34, bf16[1024,1024]{1,0:T(8,128)(2,1)S(1)} %constant_dynamic-update-slice_fusion.3, bf16[1024,512]{1,0:T(8,128)(2,1)} %collective-permute-done.3, bf16[1024,512]{1,0:T(8,128)(2,1)} %bitcast.36), kind=kOutput, calls=%fused_computation.9 | convolution fusion | flops 4312793088 | bytes 10485760 | tf_op jit(solution)/shard_map/dot_general | solution.py:72
  82.4 74.8 %reduce-scatter.2.cloned.1.call-done = f32[256,1024]{1,0:T(8,128)} async-done(((f32[1024,1024]{1,0:T(8,128)}), f32[256,1024]{1,0:T(8,128)}) %reduce-scatter.2.cloned.1.call-update) | async-done | bytes 1048592 | tf_op jit(solution)/shard_map/reduce_scatter | solution.py:71
  157.2 2.2 %fusion.30 = bf16[256,1024]{1,0:T(8,128)(2,1)} fusion(f32[256,1024]{1,0:T(8,128)} %reduce-scatter.2.cloned.1.call-done, bf16[16,16,1024]{2,1,0:T(8,128)(2,1)S(1)} %all-to-all-done.1), kind=kLoop, calls=%fused_computation.34 | loop fusion | flops 786432 | bytes 2097152 | tf_op jit(solution)/shard_map/convert_element_type | solution.py:77
  159.4 5.4 %all-to-all-start.2 = ((bf16[16,16,1024]{2,1,0:T(8,128)(2,1)}), bf16[16,16,1024]{2,1,0:T(8,128)(2,1)S(1)}, u32[]{:S(2)}, u32[]{:S(2)}) async-start(bf16[16,16,1024]{2,1,0:T(8,128)(2,1)} %bitcast.7), calls=%async_computation.3 | async-start | bytes 1048576 | tf_op jit(solution)/shard_map/all_to_all | solution.py:78
  165.3 0.7 all_to_all.15
  166.0 14.4 %all-to-all-done.2 = bf16[16,16,1024]{2,1,0:T(8,128)(2,1)S(1)} async-done(((bf16[16,16,1024]{2,1,0:T(8,128)(2,1)}), bf16[16,16,1024]{2,1,0:T(8,128)(2,1)S(1)}, u32[]{:S(2)}, u32[]{:S(2)}) %all-to-all-start.2) | async-done | bytes 524320 | tf_op jit(solution)/shard_map/all_to_all | solution.py:78
  180.4 3.5 %all-to-all-start = ((s32[16,1,8]{2,1,0:T(1,128)}), s32[16,1,8]{2,1,0:T(1,128)S(1)}, u32[]{:S(2)}, u32[]{:S(2)}) async-start(s32[16,1,8]{2,1,0:T(1,128)} %bitcast), calls=%async_computation | async-start | bytes 16384 | tf_op jit(solution)/shard_map/all_to_all | solution.py:109
  183.9 1.1 fusion.25
  185.0 5.1 %all-to-all-done = s32[16,1,8]{2,1,0:T(1,128)S(1)} async-done(((s32[16,1,8]{2,1,0:T(1,128)}), s32[16,1,8]{2,1,0:T(1,128)S(1)}, u32[]{:S(2)}, u32[]{:S(2)}) %all-to-all-start) | async-done | bytes 544 | tf_op jit(solution)/shard_map/all_to_all | solution.py:109
  190.1 3.5 %all-to-all-start.3 = ((bf16[16,8,1024]{2,1,0:T(8,128)(2,1)}), bf16[16,8,1024]{2,1,0:T(8,128)(2,1)S(1)}, u32[]{:S(2)}, u32[]{:S(2)}) async-start(bf16[16,8,1024]{2,1,0:T(8,128)(2,1)} %fusion.25), calls=%async_computation.4 | async-start | bytes 524288 | tf_op jit(solution)/shard_map/all_to_all | solution.py:102
  194.9 8.7 %all-to-all-done.3 = bf16[16,8,1024]{2,1,0:T(8,128)(2,1)S(1)} async-done(((bf16[16,8,1024]{2,1,0:T(8,128)(2,1)}), bf16[16,8,1024]{2,1,0:T(8,128)(2,1)S(1)}, u32[]{:S(2)}, u32[]{:S(2)}) %all-to-all-start.3) | async-done | bytes 262176 | tf_op jit(solution)/shard_map/all_to_all | solution.py:102
  204.0 0.9 fusion.26
  (36 shorter events, 4.4 us)
Async XLA Ops:
  7.2 2.5 %copy-start = (bf16[128,1024]{1,0:T(8,128)(2,1)S(1)}, bf16[128,1024]{1,0:T(8,128)(2,1)}, u32[]{:S(2)}) copy-start(bf16[128,1024]{1,0:T(8,128)(2,1)} %param.8) | copy-start | bytes 786436
  7.2 11.0 %copy-start.2 = (f32[2,1024]{1,0:T(2,128)S(1)}, f32[2,1024]{1,0:T(2,128)}, u32[]{:S(2)}) copy-start(f32[2,1024]{1,0:T(2,128)} %param.11) | copy-start | bytes 24580
  10.8 23.1 %all-to-all-start.1 = ((bf16[16,16,1024]{2,1,0:T(8,128)(2,1)}), bf16[16,16,1024]{2,1,0:T(8,128)(2,1)S(1)}, u32[]{:S(2)}, u32[]{:S(2)}) async-start(bf16[16,16,1024]{2,1,0:T(8,128)(2,1)} %bitcast.2), calls=%async_computation.1 | async-start | bytes 1048576 | tf_op jit(solution)/shard_map/all_to_all | solution.py:55
  18.2 139.0 %reduce-scatter.2.cloned.1.call-start = ((), (), s32[]{:S(2)}) async-start(), calls=%async_computation.5 | async-start | bytes 5242880 | tf_op jit(solution)/shard_map/reduce_scatter | solution.py:71
  34.6 16.8 %collective-permute-start = (bf16[256,1024]{1,0:T(8,128)(2,1)S(1)}, bf16[256,1024]{1,0:T(8,128)(2,1)}, u32[]{:S(2)}, u32[]{:S(2)}) collective-permute-start(bf16[256,1024]{1,0:T(8,128)(2,1)S(1)} %get-tuple-element.5), channel_id=1, source_target_pairs={{0,1},{1,2},{2,3},{3,0},{4,5},{5,6},{6,7},{7,4},{8,9},{9,10},{10,1... | collective-permute-start | bytes 1572872 | tf_op jit(solution)/shard_map/ppermute | solution.py:13
  34.7 39.0 %collective-permute-start.3 = (bf16[1024,512]{1,0:T(8,128)(2,1)}, bf16[1024,512]{1,0:T(8,128)(2,1)}, u32[]{:S(2)}, u32[]{:S(2)}) collective-permute-start(bf16[1024,512]{1,0:T(8,128)(2,1)} %bitcast.35), channel_id=1, source_target_pairs={{0,4},{4,0},{8,12},{12,8},{1,5},{5,1},{9,13},{13,9},{2,6},{6,2},{1... | collective-permute-start | bytes 3145736 | tf_op jit(solution)/shard_map/ppermute | solution.py:24
  34.7 38.9 %collective-permute-start.4 = (bf16[512,1024]{1,0:T(8,128)(2,1)}, bf16[512,1024]{1,0:T(8,128)(2,1)}, u32[]{:S(2)}, u32[]{:S(2)}) collective-permute-start(bf16[512,1024]{1,0:T(8,128)(2,1)} %bitcast.33), channel_id=1, source_target_pairs={{0,4},{4,0},{8,12},{12,8},{1,5},{5,1},{9,13},{13,9},{2,6},{6,2},{1... | collective-permute-start | bytes 3145736 | tf_op jit(solution)/shard_map/ppermute | solution.py:24
  35.2 25.7 %collective-permute-start.1 = (bf16[256,1024]{1,0:T(8,128)(2,1)S(1)}, bf16[256,1024]{1,0:T(8,128)(2,1)}, u32[]{:S(2)}, u32[]{:S(2)}) collective-permute-start(bf16[256,1024]{1,0:T(8,128)(2,1)S(1)} %get-tuple-element.5), channel_id=1, source_target_pairs={{0,3},{1,0},{2,1},{3,2},{4,7},{5,4},{6,5},{7,6},{8,11},{9,8},{10,9... | collective-permute-start | bytes 1572872 | tf_op jit(solution)/shard_map/ppermute | solution.py:16
  51.4 21.2 %collective-permute-start.2 = (bf16[256,1024]{1,0:T(8,128)(2,1)}, bf16[256,1024]{1,0:T(8,128)(2,1)}, u32[]{:S(2)}, u32[]{:S(2)}) collective-permute-start(bf16[256,1024]{1,0:T(8,128)(2,1)} %collective-permute-done), channel_id=1, source_target_pairs={{0,1},{1,2},{2,3},{3,0},{4,5},{5,6},{6,7},{7,4},{8,9},{9,10},{10,1... | collective-permute-start | bytes 1572872 | tf_op jit(solution)/shard_map/ppermute | solution.py:13
  159.4 44.7 %copy-start.3 = (bf16[1024,128]{1,0:T(8,128)(2,1)S(1)}, bf16[1024,128]{1,0:T(8,128)(2,1)}, u32[]{:S(2)}) copy-start(bf16[1024,128]{1,0:T(8,128)(2,1)} %param.15) | copy-start | bytes 786436
  159.4 44.7 %copy-start.4 = (f32[1024]{0:T(1024)S(1)}, f32[1024]{0:T(1024)}, u32[]{:S(2)}) copy-start(f32[1024]{0:T(1024)} %param.14) | copy-start | bytes 12292
  159.4 21.1 %all-to-all-start.2 = ((bf16[16,16,1024]{2,1,0:T(8,128)(2,1)}), bf16[16,16,1024]{2,1,0:T(8,128)(2,1)S(1)}, u32[]{:S(2)}, u32[]{:S(2)}) async-start(bf16[16,16,1024]{2,1,0:T(8,128)(2,1)} %bitcast.7), calls=%async_computation.3 | async-start | bytes 1048576 | tf_op jit(solution)/shard_map/all_to_all | solution.py:78
  180.4 9.7 %all-to-all-start = ((s32[16,1,8]{2,1,0:T(1,128)}), s32[16,1,8]{2,1,0:T(1,128)S(1)}, u32[]{:S(2)}, u32[]{:S(2)}) async-start(s32[16,1,8]{2,1,0:T(1,128)} %bitcast), calls=%async_computation | async-start | bytes 16384 | tf_op jit(solution)/shard_map/all_to_all | solution.py:109
  190.1 13.6 %all-to-all-start.3 = ((bf16[16,8,1024]{2,1,0:T(8,128)(2,1)}), bf16[16,8,1024]{2,1,0:T(8,128)(2,1)S(1)}, u32[]{:S(2)}, u32[]{:S(2)}) async-start(bf16[16,8,1024]{2,1,0:T(8,128)(2,1)} %fusion.25), calls=%async_computation.4 | async-start | bytes 524288 | tf_op jit(solution)/shard_map/all_to_all | solution.py:102
  204.0 1.0 copy-start.1
Sparse Core Ops, SparseCore 0:
  82.5 74.6 reduce-scatter.1
